TPU v7x, 128 devices: a whole 4x4x4 slice. The times are simulated.
128 devices in a mesh: row: 8 (over z, core), col: 16 (over x, y).
Axes of the slice: x: 4, y: 4, z: 4, core: 2. Of those that a mesh axis runs over, the one named last changes fastest.
Arguments:
- updates: float32 [16384, 8192], P('col', 'row'), may hold values from -6 to 6
- block_map: int32 [2, 64], replicated, may hold values from 0 to 79, as said below
- own_diag: float32 [10240], P('row'), may hold values from 2 to 6
- panel_inverse: float32 [512, 512], replicated, as said below
Outputs:
- factor_panel: float32 [10240, 512], P('row')
- trailing: float32 [10240, 10240], P('row', 'col')
Inputs may be any that keep to these rules, and one draw needn't show every extreme that they name: `block_map`: within one child the 64 entries name distinct front blocks. Take the child blocks (a, b) held by one device in updates, and the front blocks held by one device in trailing: either exactly 1 of the former land in the latter, or none do. `panel_inverse`: lower triangular with a positive diagonal.
All inputs are finite; a program needn't handle non-finite values.
Results may differ from a plain program's by a relative error of at most 0.000075.
Values sent between devices are 32-bit elements; how exact they have to be, the bound alone decides.
No kernel may reach another device: no remote copies, remote signals or barrier semaphores. Data moves between devices by JAX's collectives and lax.ppermute only.
A program may use at most 128 MiB of HBM per device.

v0:
```python
import jax
import jax.numpy as jnp
from jax import lax
from jax.sharding import PartitionSpec as P

F = 10240
M = 8192
BLK = 128
PANEL = 512


def on_device(updates, block_map, own_diag, panel_inverse):
    row_count = lax.axis_size("row")
    col_count = lax.axis_size("col")
    row_index = lax.axis_index("row")
    col_index = lax.axis_index("col")
    devices_all = row_count * col_count
    local_rows, local_cols = updates.shape
    row_items = local_rows // BLK
    col_items = local_cols // BLK
    half_cols = col_count // 2
    front_blocks = F // BLK
    front_rows = front_blocks // row_count
    front_cols = front_blocks // col_count
    height = front_rows * BLK
    col_width = front_cols * BLK
    block_map = block_map.astype(jnp.int32)
    child = col_index // half_cols
    child_map = jnp.take(block_map, child, axis=0)
    row_parent = lax.dynamic_slice_in_dim(child_map, col_index % half_cols * row_items, row_items)
    col_parent = lax.dynamic_slice_in_dim(child_map, row_index * col_items, col_items)
    inv_k = (
        jnp.zeros((row_count,), jnp.int32)
        .at[row_parent // front_rows]
        .set(jnp.arange(row_items, dtype=jnp.int32))
    )
    inv_l = (
        jnp.full((col_count,), -1, jnp.int32)
        .at[col_parent // front_cols]
        .set(jnp.arange(col_items, dtype=jnp.int32))
    )
    fill_l = jnp.where(inv_l >= 0, inv_l, col_items)
    outgoing = (
        updates.reshape(row_items, BLK, col_items, BLK)
        .at[inv_k[:, None], :, fill_l[None, :], :]
        .get(mode="fill", fill_value=0.0)
        .reshape(devices_all, 1, BLK, BLK)
    )
    incoming = lax.all_to_all(
        outgoing, ("row", "col"), split_axis=0, concat_axis=0, tiled=True
    ).reshape(devices_all, BLK, BLK)
    my_rows = row_index * front_rows + jnp.arange(front_rows, dtype=jnp.int32)
    my_cols = col_index * front_cols + jnp.arange(front_cols, dtype=jnp.int32)
    lanes = jnp.arange(BLK, dtype=jnp.int32)
    front_local = None
    for child_id in range(2):
        inverse = (
            jnp.full((front_blocks,), -1, jnp.int32)
            .at[block_map[child_id]]
            .set(jnp.arange(block_map.shape[1], dtype=jnp.int32))
        )
        a = jnp.take(inverse, my_rows)
        b = jnp.take(inverse, my_cols)
        source = (jnp.maximum(b, 0) // col_items)[None, :] * col_count + (
            child_id * half_cols + jnp.maximum(a, 0) // row_items
        )[:, None]
        valid = (a >= 0)[:, None] & (b >= 0)[None, :]
        source = jnp.where(valid, source, devices_all)
        part = incoming.at[source[:, None, :], lanes[None, :, None], :].get(
            mode="fill", fill_value=0.0
        )
        front_local = part if front_local is None else front_local + part
    front_local = front_local.reshape(height, col_width)
    row_global = row_index * height + jnp.arange(height, dtype=jnp.int32)
    col_global = col_index * col_width + jnp.arange(col_width, dtype=jnp.int32)
    front_local = front_local + jnp.where(
        row_global[:, None] == col_global[None, :], own_diag[:, None], 0.0
    )
    piece_rows = height // col_count
    raw_panel = front_local[:, :PANEL]
    piece = jnp.where(col_index == 0, raw_panel[:piece_rows], 0.0)
    for k in range(1, col_count):
        pairs = [(r * col_count, r * col_count + k) for r in range(row_count)]
        piece = piece + lax.ppermute(
            raw_panel[k * piece_rows : (k + 1) * piece_rows], ("row", "col"), pairs
        )
    factor_piece = jnp.dot(
        piece, panel_inverse.T, precision=lax.Precision.HIGHEST, preferred_element_type=jnp.float32
    )
    factor_panel = lax.all_gather(factor_piece, "col", axis=0, tiled=True)
    ratio = col_count // row_count
    pairs = [
        (r * col_count + k, k % row_count * col_count + r * ratio + k // row_count)
        for r in range(row_count)
        for k in range(col_count)
    ]
    moved = lax.ppermute(factor_piece, ("row", "col"), pairs)
    stack = [moved]
    for q in range(1, row_count):
        shift = [(r, (r + q) % row_count) for r in range(row_count)]
        stack.append(lax.ppermute(moved, "row", shift))
    order = (row_index - jnp.arange(row_count, dtype=jnp.int32)) % row_count
    across = jnp.take(jnp.stack(stack), order, axis=0).reshape(col_width, PANEL)
    update_term = lax.dot_general(
        factor_panel,
        across,
        (((1,), (1,)), ((), ())),
        precision=lax.Precision.HIGHEST,
        preferred_element_type=jnp.float32,
    )
    trailing = front_local - update_term
    return (factor_panel, trailing)


def solution(mesh):
    return jax.shard_map(
        on_device,
        mesh=mesh,
        in_specs=(P("col", "row"), P(), P("row"), P()),
        out_specs=(P("row", None), P("row", "col")),
        check_vma=False,
    )
```

profile of v0, /device:TPU:0, one launch (start us, length us, event | category | flops | bytes accessed | tf_op | source)
XLA Modules:
  0.0 391.2 jit_solution(3016989263311851734)
XLA Ops:
  9.5 3.2 copy.17
  12.7 2.7 copy.12
  15.6 6.5 %gather_fusion = f32[128,128,128]{2,1,0:T(8,128)} fusion(f32[8,128,8,128]{3,1,2,0:T(8,128)} %copy.12, s32[128]{0:T(128)S(1)} %reshape.345), kind=kCustom, calls=%fused_computation.4 | custom fusion | bytes 16778240 | tf_op jit(solution)/shard_map/gather | solution.py:46
  22.1 7.2 %fusion = f32[128,1,128,128]{3,2,1,0:T(8,128)} fusion(f32[128,128,128]{2,1,0:T(8,128)} %gather_fusion, pred[128]{0:T(512)(128)(4,1)S(1)} %broadcast_in_dim.136), kind=kLoop, calls=%fused_computation.13 | loop fusion | flops 2097152 | bytes 16777344 | tf_op jit(solution)/shard_map/select_n | solution.py:46
  29.3 11.7 %all-to-all-start = ((f32[128,1,128,128]{3,2,1,0:T(8,128)}), f32[128,1,128,128]{3,2,1,0:T(8,128)}, u32[]{:S(2)}, u32[]{:S(2)}) async-start(f32[128,1,128,128]{3,2,1,0:T(8,128)} %fusion), calls=%async_computation | async-start | bytes 16777216 | tf_op jit(solution)/shard_map/all_to_all | solution.py:49
  48.4 90.6 %all-to-all-done = f32[128,1,128,128]{3,2,1,0:T(8,128)} async-done(((f32[128,1,128,128]{3,2,1,0:T(8,128)}), f32[128,1,128,128]{3,2,1,0:T(8,128)}, u32[]{:S(2)}, u32[]{:S(2)}) %all-to-all-start) | async-done | bytes 8388640 | tf_op jit(solution)/shard_map/all_to_all | solution.py:49
  139.0 61.8 %gather_fusion.1 = f32[6400,128]{1,0:T(8,128)} fusion(f32[128,128,128]{2,1,0:T(8,128)} %bitcast.8, s32[6400]{0:T(1024)S(1)} %reshape.351), kind=kCustom, calls=%fused_computation.5 | custom fusion | bytes 6604800 | tf_op jit(solution)/shard_map/gather | solution.py:69
  200.8 4.9 %reshape.354 = f32[10,128,5,128]{3,2,1,0:T(8,128)} reshape(f32[6400,128]{1,0:T(8,128)} %gather_fusion.1) | data formatting | bytes 6553600 | tf_op jit(solution)/shard_map/gather | solution.py:69
  205.7 61.7 %gather_fusion.2 = f32[6400,128]{1,0:T(8,128)} fusion(f32[128,128,128]{2,1,0:T(8,128)} %bitcast.8, s32[6400]{0:T(1024)S(1)} %reshape.357), kind=kCustom, calls=%fused_computation.6 | custom fusion | bytes 6604800 | tf_op jit(solution)/shard_map/gather | solution.py:69
  267.4 4.9 %reshape.360 = f32[10,128,5,128]{3,2,1,0:T(8,128)} reshape(f32[6400,128]{1,0:T(8,128)} %gather_fusion.2) | data formatting | bytes 6553600 | tf_op jit(solution)/shard_map/gather | solution.py:69
  272.3 5.5 %select_add_fusion = f32[10,128,5,128]{3,2,1,0:T(8,128)S(1)} fusion(f32[10,128,5,128]{3,2,1,0:T(8,128)} %reshape.360, f32[10,128,5,128]{3,2,1,0:T(8,128)} %reshape.354, pred[10,128,5]{2,1,0:T(8,128)(4,1)S(1)} %copy.15, pred[10,128,5]{2,1,0:T(8,128)(4,1)S(1)} %copy.11), kind=kLoop, calls=%fused_computation.14 | loop fusion | flops 2457600 | bytes 9843200 | tf_op jit(solution)/shard_map/add | solution.py:72
  280.5 2.7 collective-permute-start
  283.3 3.5 collective-permute-start.1
  286.8 3.3 collective-permute-start.10
  313.3 3.3 collective-permute-done.7
  316.6 3.5 collective-permute-done.8
  322.4 3.1 fusion.16
  327.3 6.0 %collective-permute-start.16 = (f32[80,512]{1,0:T(8,128)S(1)}, f32[80,512]{1,0:T(8,128)S(1)}, u32[]{:S(2)}, u32[]{:S(2)}) collective-permute-start(f32[80,512]{1,0:T(8,128)S(1)} %collective-permute-done.15), channel_id=1, source_target_pairs={{0,16},{16,32},{32,48},{48,64},{64,80},{80,96},{96,112},{112,0},{1... | collective-permute-start | bytes 491528 | tf_op jit(solution)/shard_map/ppermute | solution.py:101
  333.4 7.3 %collective-permute-start.17 = (f32[80,512]{1,0:T(8,128)S(1)}, f32[80,512]{1,0:T(8,128)S(1)}, u32[]{:S(2)}, u32[]{:S(2)}) collective-permute-start(f32[80,512]{1,0:T(8,128)S(1)} %collective-permute-done.15), channel_id=1, source_target_pairs={{0,32},{16,48},{32,64},{48,80},{64,96},{80,112},{96,0},{112,16},{1... | collective-permute-start | bytes 491528 | tf_op jit(solution)/shard_map/ppermute | solution.py:101
  341.1 3.7 collective-permute-start.19
  346.7 2.8 collective-permute-start.22
  349.5 3.1 collective-permute-done.18
  359.6 13.5 %all-gather.2.cloned.1.call-done = f32[1280,512]{1,0:T(8,128)} async-done(((f32[80,512]{1,0:T(8,128)}), f32[1280,512]{1,0:T(8,128)}) %all-gather.2.cloned.1.call-update) | async-done | bytes 2621456 | tf_op jit(solution)/shard_map/all_gather | solution.py:90
  373.1 9.8 %convolution_subtract_fusion = f32[1280,640]{1,0:T(8,128)} fusion(f32[1280,640]{1,0:T(8,128)} %copy-done.1, f32[1280,512]{1,0:T(8,128)} %all-gather.2.cloned.1.call-done, f32[640,512]{1,0:T(8,128)S(1)} %bitcast_select_fusion.1), kind=kOutput, calls=%fused_computation.15 | convolution fusion | flops 5033984000 | bytes 10485760 | tf_op jit(solution)/shard_map/dot_general | solution.py:104
  (113 shorter events, 50.3 us)
Async XLA Ops:
  29.3 109.8 %all-to-all-start = ((f32[128,1,128,128]{3,2,1,0:T(8,128)}), f32[128,1,128,128]{3,2,1,0:T(8,128)}, u32[]{:S(2)}, u32[]{:S(2)}) async-start(f32[128,1,128,128]{3,2,1,0:T(8,128)} %fusion), calls=%async_computation | async-start | bytes 16777216 | tf_op jit(solution)/shard_map/all_to_all | solution.py:49
  41.0 332.1 %all-gather.2.cloned.1.call-start = ((), (), s32[]{:S(2)}) async-start(), calls=%async_computation.1 | async-start | bytes 2785280 | tf_op jit(solution)/shard_map/all_gather | solution.py:90
  280.5 12.2 %collective-permute-start = (f32[80,512]{1,0:T(8,128)S(1)}, f32[80,512]{1,0:T(8,128)S(1)}, u32[]{:S(2)}, u32[]{:S(2)}) collective-permute-start(f32[80,512]{1,0:T(8,128)S(1)} %get-tuple-element.19), channel_id=1, source_target_pairs={{0,1},{16,17},{32,33},{48,49},{64,65},{80,81},{96,97},{112,113}} | collective-permute-start | bytes 491528 | tf_op jit(solution)/shard_map/ppermute | solution.py:84
  283.3 10.8 %collective-permute-start.1 = (f32[80,512]{1,0:T(8,128)S(1)}, f32[80,512]{1,0:T(8,128)S(1)}, u32[]{:S(2)}, u32[]{:S(2)}) collective-permute-start(f32[80,512]{1,0:T(8,128)S(1)} %get-tuple-element.33), channel_id=1, source_target_pairs={{0,2},{16,18},{32,34},{48,50},{64,66},{80,82},{96,98},{112,114}} | collective-permute-start | bytes 491528 | tf_op jit(solution)/shard_map/ppermute | solution.py:84
  286.8 8.6 %collective-permute-start.10 = (f32[80,512]{1,0:T(8,128)S(1)}, f32[80,512]{1,0:T(8,128)S(1)}, u32[]{:S(2)}, u32[]{:S(2)}) collective-permute-start(f32[80,512]{1,0:T(8,128)S(1)} %get-tuple-element.24), channel_id=1, source_target_pairs={{0,11},{16,27},{32,43},{48,59},{64,75},{80,91},{96,107},{112,123}} | collective-permute-start | bytes 491528 | tf_op jit(solution)/shard_map/ppermute | solution.py:84
  290.1 6.6 %collective-permute-start.11 = (f32[80,512]{1,0:T(8,128)S(1)}, f32[80,512]{1,0:T(8,128)S(1)}, u32[]{:S(2)}, u32[]{:S(2)}) collective-permute-start(f32[80,512]{1,0:T(8,128)S(1)} %get-tuple-element.23), channel_id=1, source_target_pairs={{0,12},{16,28},{32,44},{48,60},{64,76},{80,92},{96,108},{112,124}} | collective-permute-start | bytes 491528 | tf_op jit(solution)/shard_map/ppermute | solution.py:84
  291.4 8.1 %collective-permute-start.12 = (f32[80,512]{1,0:T(8,128)S(1)}, f32[80,512]{1,0:T(8,128)S(1)}, u32[]{:S(2)}, u32[]{:S(2)}) collective-permute-start(f32[80,512]{1,0:T(8,128)S(1)} %get-tuple-element.22), channel_id=1, source_target_pairs={{0,13},{16,29},{32,45},{48,61},{64,77},{80,93},{96,109},{112,125}} | collective-permute-start | bytes 491528 | tf_op jit(solution)/shard_map/ppermute | solution.py:84
  292.7 10.3 %collective-permute-start.13 = (f32[80,512]{1,0:T(8,128)S(1)}, f32[80,512]{1,0:T(8,128)S(1)}, u32[]{:S(2)}, u32[]{:S(2)}) collective-permute-start(f32[80,512]{1,0:T(8,128)S(1)} %get-tuple-element.21), channel_id=1, source_target_pairs={{0,14},{16,30},{32,46},{48,62},{64,78},{80,94},{96,110},{112,126}} | collective-permute-start | bytes 491528 | tf_op jit(solution)/shard_map/ppermute | solution.py:84
  294.0 11.2 %collective-permute-start.14 = (f32[80,512]{1,0:T(8,128)S(1)}, f32[80,512]{1,0:T(8,128)S(1)}, u32[]{:S(2)}, u32[]{:S(2)}) collective-permute-start(f32[80,512]{1,0:T(8,128)S(1)} %get-tuple-element.20), channel_id=1, source_target_pairs={{0,15},{16,31},{32,47},{48,63},{64,79},{80,95},{96,111},{112,127}} | collective-permute-start | bytes 491528 | tf_op jit(solution)/shard_map/ppermute | solution.py:84
  295.4 12.1 %collective-permute-start.2 = (f32[80,512]{1,0:T(8,128)S(1)}, f32[80,512]{1,0:T(8,128)S(1)}, u32[]{:S(2)}, u32[]{:S(2)}) collective-permute-start(f32[80,512]{1,0:T(8,128)S(1)} %get-tuple-element.32), channel_id=1, source_target_pairs={{0,3},{16,19},{32,35},{48,51},{64,67},{80,83},{96,99},{112,115}} | collective-permute-start | bytes 491528 | tf_op jit(solution)/shard_map/ppermute | solution.py:84
  296.7 12.7 %collective-permute-start.3 = (f32[80,512]{1,0:T(8,128)S(1)}, f32[80,512]{1,0:T(8,128)S(1)}, u32[]{:S(2)}, u32[]{:S(2)}) collective-permute-start(f32[80,512]{1,0:T(8,128)S(1)} %get-tuple-element.31), channel_id=1, source_target_pairs={{0,4},{16,20},{32,36},{48,52},{64,68},{80,84},{96,100},{112,116}} | collective-permute-start | bytes 491528 | tf_op jit(solution)/shard_map/ppermute | solution.py:84
  299.5 11.8 %collective-permute-start.4 = (f32[80,512]{1,0:T(8,128)S(1)}, f32[80,512]{1,0:T(8,128)S(1)}, u32[]{:S(2)}, u32[]{:S(2)}) collective-permute-start(f32[80,512]{1,0:T(8,128)S(1)} %get-tuple-element.30), channel_id=1, source_target_pairs={{0,5},{16,21},{32,37},{48,53},{64,69},{80,85},{96,101},{112,117}} | collective-permute-start | bytes 491528 | tf_op jit(solution)/shard_map/ppermute | solution.py:84
  303.0 10.3 %collective-permute-start.5 = (f32[80,512]{1,0:T(8,128)S(1)}, f32[80,512]{1,0:T(8,128)}, u32[]{:S(2)}, u32[]{:S(2)}) collective-permute-start(f32[80,512]{1,0:T(8,128)S(1)} %get-tuple-element.29), channel_id=1, source_target_pairs={{0,6},{16,22},{32,38},{48,54},{64,70},{80,86},{96,102},{112,118}} | collective-permute-start | bytes 491528 | tf_op jit(solution)/shard_map/ppermute | solution.py:84
  305.3 8.0 %collective-permute-start.6 = (f32[80,512]{1,0:T(8,128)S(1)}, f32[80,512]{1,0:T(8,128)}, u32[]{:S(2)}, u32[]{:S(2)}) collective-permute-start(f32[80,512]{1,0:T(8,128)S(1)} %get-tuple-element.28), channel_id=1, source_target_pairs={{0,7},{16,23},{32,39},{48,55},{64,71},{80,87},{96,103},{112,119}} | collective-permute-start | bytes 491528 | tf_op jit(solution)/shard_map/ppermute | solution.py:84
  307.4 9.2 %collective-permute-start.7 = (f32[80,512]{1,0:T(8,128)S(1)}, f32[80,512]{1,0:T(8,128)}, u32[]{:S(2)}, u32[]{:S(2)}) collective-permute-start(f32[80,512]{1,0:T(8,128)S(1)} %get-tuple-element.27), channel_id=1, source_target_pairs={{0,8},{16,24},{32,40},{48,56},{64,72},{80,88},{96,104},{112,120}} | collective-permute-start | bytes 491528 | tf_op jit(solution)/shard_map/ppermute | solution.py:84
  309.4 10.7 %collective-permute-start.8 = (f32[80,512]{1,0:T(8,128)S(1)}, f32[80,512]{1,0:T(8,128)}, u32[]{:S(2)}, u32[]{:S(2)}) collective-permute-start(f32[80,512]{1,0:T(8,128)S(1)} %get-tuple-element.26), channel_id=1, source_target_pairs={{0,9},{16,25},{32,41},{48,57},{64,73},{80,89},{96,105},{112,121}} | collective-permute-start | bytes 491528 | tf_op jit(solution)/shard_map/ppermute | solution.py:84
  311.3 11.1 %collective-permute-start.9 = (f32[80,512]{1,0:T(8,128)S(1)}, f32[80,512]{1,0:T(8,128)}, u32[]{:S(2)}, u32[]{:S(2)}) collective-permute-start(f32[80,512]{1,0:T(8,128)S(1)} %get-tuple-element.25), channel_id=1, source_target_pairs={{0,10},{16,26},{32,42},{48,58},{64,74},{80,90},{96,106},{112,122}} | collective-permute-start | bytes 491528 | tf_op jit(solution)/shard_map/ppermute | solution.py:84
  327.3 17.5 %collective-permute-start.16 = (f32[80,512]{1,0:T(8,128)S(1)}, f32[80,512]{1,0:T(8,128)S(1)}, u32[]{:S(2)}, u32[]{:S(2)}) collective-permute-start(f32[80,512]{1,0:T(8,128)S(1)} %collective-permute-done.15), channel_id=1, source_target_pairs={{0,16},{16,32},{32,48},{48,64},{64,80},{80,96},{96,112},{112,0},{1... | collective-permute-start | bytes 491528 | tf_op jit(solution)/shard_map/ppermute | solution.py:101
  333.4 13.3 %collective-permute-start.17 = (f32[80,512]{1,0:T(8,128)S(1)}, f32[80,512]{1,0:T(8,128)S(1)}, u32[]{:S(2)}, u32[]{:S(2)}) collective-permute-start(f32[80,512]{1,0:T(8,128)S(1)} %collective-permute-done.15), channel_id=1, source_target_pairs={{0,32},{16,48},{32,64},{48,80},{64,96},{80,112},{96,0},{112,16},{1... | collective-permute-start | bytes 491528 | tf_op jit(solution)/shard_map/ppermute | solution.py:101
  340.6 11.9 %collective-permute-start.18 = (f32[80,512]{1,0:T(8,128)S(1)}, f32[80,512]{1,0:T(8,128)S(1)}, u32[]{:S(2)}, u32[]{:S(2)}) collective-permute-start(f32[80,512]{1,0:T(8,128)S(1)} %collective-permute-done.15), channel_id=1, source_target_pairs={{0,48},{16,64},{32,80},{48,96},{64,112},{80,0},{96,16},{112,32},{1... | collective-permute-start | bytes 491528 | tf_op jit(solution)/shard_map/ppermute | solution.py:101
  341.1 12.7 %collective-permute-start.19 = (f32[80,512]{1,0:T(8,128)S(1)}, f32[80,512]{1,0:T(8,128)S(1)}, u32[]{:S(2)}, u32[]{:S(2)}) collective-permute-start(f32[80,512]{1,0:T(8,128)S(1)} %collective-permute-done.15), channel_id=1, source_target_pairs={{0,64},{16,80},{32,96},{48,112},{64,0},{80,16},{96,32},{112,48},{1... | collective-permute-start | bytes 491528 | tf_op jit(solution)/shard_map/ppermute | solution.py:101
  344.8 10.4 %collective-permute-start.20 = (f32[80,512]{1,0:T(8,128)S(1)}, f32[80,512]{1,0:T(8,128)S(1)}, u32[]{:S(2)}, u32[]{:S(2)}) collective-permute-start(f32[80,512]{1,0:T(8,128)S(1)} %collective-permute-done.15), channel_id=1, source_target_pairs={{0,80},{16,96},{32,112},{48,0},{64,16},{80,32},{96,48},{112,64},{1... | collective-permute-start | bytes 491528 | tf_op jit(solution)/shard_map/ppermute | solution.py:101
  344.8 10.9 %collective-permute-start.21 = (f32[80,512]{1,0:T(8,128)S(1)}, f32[80,512]{1,0:T(8,128)S(1)}, u32[]{:S(2)}, u32[]{:S(2)}) collective-permute-start(f32[80,512]{1,0:T(8,128)S(1)} %collective-permute-done.15), channel_id=1, source_target_pairs={{0,96},{16,112},{32,0},{48,16},{64,32},{80,48},{96,64},{112,80},{1... | collective-permute-start | bytes 491528 | tf_op jit(solution)/shard_map/ppermute | solution.py:101
  346.7 9.7 %collective-permute-start.22 = (f32[80,512]{1,0:T(8,128)S(1)}, f32[80,512]{1,0:T(8,128)S(1)}, u32[]{:S(2)}, u32[]{:S(2)}) collective-permute-start(f32[80,512]{1,0:T(8,128)S(1)} %collective-permute-done.15), channel_id=1, source_target_pairs={{0,112},{16,0},{32,16},{48,32},{64,48},{80,64},{96,80},{112,96},{1... | collective-permute-start | bytes 491528 | tf_op jit(solution)/shard_map/ppermute | solution.py:101
  (6 other events, 345.8 us)
Sparse Core Ops, SparseCore 0:
  325.7 47.3 all-gather.1
where the time goes:
time: 393 us; the launch traced here: 391 us
  local copies, waits for them, and re-layouts  159 us (40%)
  waiting for transfers between devices  124 us (32%)
  starting transfers between devices  63.9 us (16%)
  other arithmetic  16.6 us (4%)
  between operations  14.6 us (4%)
  matrix products  12.9 us (3%)
    gather x4, local copies, waits for them, and re-layouts, on_device(): incoming.at[source[:, None, :], lanes[None, :, None], :]  133 us
    all_to_all x1, waiting for transfers between devices, on_device(): lax.all_to_all(outgoing, ('row', 'col'), split_axis=0, concat_axis=0, til...  90.6 us
    ppermute x15, starting transfers between devices, on_device(): lax.ppermute(raw_panel[k * piece_rows:(k + 1) * piece_rows], ('row', 'col...  28.6 us
    ppermute x7, starting transfers between devices, on_device(): stack.append(lax.ppermute(moved, 'row', shift))  22 us
    all_gather x1, waiting for transfers between devices, on_device(): factor_panel = lax.all_gather(factor_piece, 'col', axis=0, tiled=True)  13.5 us
    ppermute x15, waiting for transfers between devices, on_device(): lax.ppermute(raw_panel[k * piece_rows:(k + 1) * piece_rows], ('row', 'col...  13.2 us
    all_to_all x1, starting transfers between devices, on_device(): lax.all_to_all(outgoing, ('row', 'col'), split_axis=0, concat_axis=0, til...  11.7 us
    dot_general x1, matrix products, on_device(): lax.dot_general(factor_panel, across, (((1,), (1,)), ((), ())), precision...  9.78 us
  transfers between devices with their start and end apart: 25, of which 13 were waited for; matrix products, arithmetic and copies ran while one was open for 3% of the time, Pallas kernels for 0%

commit v1 on v0

--- a/solution.py
+++ b/solution.py
@@ -7,6 +7,28 @@
 M = 8192
 BLK = 128
 PANEL = 512
+
+
+def in_order(pieces, dim):
+    dims = list(pieces.shape[1:])
+    dims[dim] *= pieces.shape[0]
+    return jnp.moveaxis(pieces, 0, dim).reshape(dims)
+
+
+def ring_gather(x, axis, dim):
+    length = lax.axis_size(axis)
+    pairs = [(i, (i + 1) % length) for i in range(length)]
+    back = [(b, a) for a, b in pairs]
+    lower, upper = ([], [])
+    for step in range(length - 1):
+        if step % 2 == 0:
+            lower.append(lax.ppermute(lower[-1] if lower else x, axis, pairs))
+        else:
+            upper.append(lax.ppermute(upper[-1] if upper else x, axis, back))
+    blocks = jnp.stack([*lower[::-1], x, *upper])
+    shift = lax.axis_index(axis) - len(lower)
+    blocks = blocks[(jnp.arange(length) - shift) % length]
+    return in_order(blocks, dim)
 
 
 def on_device(updates, block_map, own_diag, panel_inverse):
@@ -87,7 +109,7 @@
     factor_piece = jnp.dot(
         piece, panel_inverse.T, precision=lax.Precision.HIGHEST, preferred_element_type=jnp.float32
     )
-    factor_panel = lax.all_gather(factor_piece, "col", axis=0, tiled=True)
+    factor_panel = ring_gather(factor_piece, "col", 0)
     ratio = col_count // row_count
     pairs = [
         (r * col_count + k, k % row_count * col_count + r * ratio + k // row_count)

time: 393 us -> 435 us (1.11)
  starting transfers between devices: 63.9 us -> 93.8 us
  local copies, waits for them, and re-layouts: 159 us -> 176 us
  between operations: 14.6 us -> 1.33 us
  waiting for transfers between devices: 124 us -> 134 us
    ppermute x0 -> x15, starting transfers between devices: none -> 33.6 us  [the longest x7 31.7 us: ring_gather(): upper.append(lax.ppermute(upper[-1] if upper else x, axis, back))]
    ppermute x0 -> x15, waiting for transfers between devices: none -> 26.4 us  [the longest x8 26 us: ring_gather(): lower.append(lax.ppermute(lower[-1] if lower else x, axis, pairs))]
    all_gather x1 -> x0, waiting for transfers between devices: 13.5 us -> none  [on_device(): factor_panel = lax.all_gather(factor_piece, 'col', axis=0, tiled=True)]
    unnamed x19 -> x39, local copies, waits for them, and re-layouts: 6.5 us -> 18.8 us
  transfers between devices with their start and end apart: 25 -> 39, of which waited for: 13 -> 16; matrix products, arithmetic and copies ran while one was open for 3% -> 6% of each run, Pallas kernels for 0% -> 0%
where the time goes in v1:
time: 435 us; the launch traced here: 434 us
  local copies, waits for them, and re-layouts  176 us (40%)
  waiting for transfers between devices  134 us (31%)
  starting transfers between devices  93.8 us (22%)
  other arithmetic  16.8 us (4%)
  matrix products  12.1 us (3%)
    gather x4, local copies, waits for them, and re-layouts, on_device(): incoming.at[source[:, None, :], lanes[None, :, None], :]  133 us
    all_to_all x1, waiting for transfers between devices, on_device(): lax.all_to_all(outgoing, ('row', 'col'), split_axis=0, concat_axis=0, til...  90.7 us
    ppermute x7, starting transfers between devices, ring_gather(): upper.append(lax.ppermute(upper[-1] if upper else x, axis, back))  31.7 us
    ppermute x15, starting transfers between devices, on_device(): lax.ppermute(raw_panel[k * piece_rows:(k + 1) * piece_rows], ('row', 'col...  28.5 us
    ppermute x8, waiting for transfers between devices, ring_gather(): lower.append(lax.ppermute(lower[-1] if lower else x, axis, pairs))  26 us
    ppermute x7, starting transfers between devices, on_device(): stack.append(lax.ppermute(moved, 'row', shift))  19.3 us
    unnamed x39, local copies, waits for them, and re-layouts  18.8 us
    ppermute x15, waiting for transfers between devices, on_device(): lax.ppermute(raw_panel[k * piece_rows:(k + 1) * piece_rows], ('row', 'col...  13.1 us
  transfers between devices with their start and end apart: 39, of which 16 were waited for; matrix products, arithmetic and copies ran while one was open for 6% of the time, Pallas kernels for 0%

profile of v1, /device:TPU:0, one launch (start us, length us, event | category | flops | bytes accessed | tf_op | source)
XLA Modules:
  0.0 433.8 jit_solution(6083016939844018700)
XLA Ops:
  9.1 6.5 %gather_fusion = f32[128,128,128]{2,1,0:T(8,128)} fusion(f32[8,128,8,128]{3,1,2,0:T(8,128)} %copy.12, s32[128]{0:T(128)S(1)} %reshape.428), kind=kCustom, calls=%fused_computation.4 | custom fusion | bytes 16778240 | tf_op jit(solution)/shard_map/gather | solution.py:68
  15.6 7.2 %fusion = f32[128,1,128,128]{3,2,1,0:T(8,128)} fusion(f32[128,128,128]{2,1,0:T(8,128)} %gather_fusion, pred[128]{0:T(512)(128)(4,1)S(1)} %broadcast_in_dim.133), kind=kLoop, calls=%fused_computation.14 | loop fusion | flops 2097152 | bytes 16777344 | tf_op jit(solution)/shard_map/select_n | solution.py:68
  22.8 11.7 %all-to-all-start = ((f32[128,1,128,128]{3,2,1,0:T(8,128)}), f32[128,1,128,128]{3,2,1,0:T(8,128)}, u32[]{:S(2)}, u32[]{:S(2)}) async-start(f32[128,1,128,128]{3,2,1,0:T(8,128)} %fusion), calls=%async_computation | async-start | bytes 16777216 | tf_op jit(solution)/shard_map/all_to_all | solution.py:71
  41.9 90.7 %all-to-all-done = f32[128,1,128,128]{3,2,1,0:T(8,128)} async-done(((f32[128,1,128,128]{3,2,1,0:T(8,128)}), f32[128,1,128,128]{3,2,1,0:T(8,128)}, u32[]{:S(2)}, u32[]{:S(2)}) %all-to-all-start) | async-done | bytes 8388640 | tf_op jit(solution)/shard_map/all_to_all | solution.py:71
  132.6 61.7 %gather_fusion.1 = f32[6400,128]{1,0:T(8,128)} fusion(f32[128,128,128]{2,1,0:T(8,128)} %bitcast.8, s32[6400]{0:T(1024)S(1)} %reshape.434), kind=kCustom, calls=%fused_computation.5 | custom fusion | bytes 6604800 | tf_op jit(solution)/shard_map/gather | solution.py:91
  194.2 4.8 %reshape.437 = f32[10,128,5,128]{3,2,1,0:T(8,128)} reshape(f32[6400,128]{1,0:T(8,128)} %gather_fusion.1) | data formatting | bytes 6553600 | tf_op jit(solution)/shard_map/gather | solution.py:91
  199.1 61.7 %gather_fusion.2 = f32[6400,128]{1,0:T(8,128)} fusion(f32[128,128,128]{2,1,0:T(8,128)} %bitcast.8, s32[6400]{0:T(1024)S(1)} %reshape.440), kind=kCustom, calls=%fused_computation.6 | custom fusion | bytes 6604800 | tf_op jit(solution)/shard_map/gather | solution.py:91
  260.8 4.9 %reshape.443 = f32[10,128,5,128]{3,2,1,0:T(8,128)} reshape(f32[6400,128]{1,0:T(8,128)} %gather_fusion.2) | data formatting | bytes 6553600 | tf_op jit(solution)/shard_map/gather | solution.py:91
  265.7 5.5 %select_add_fusion = f32[10,128,5,128]{3,2,1,0:T(8,128)S(1)} fusion(f32[10,128,5,128]{3,2,1,0:T(8,128)} %reshape.443, f32[10,128,5,128]{3,2,1,0:T(8,128)} %reshape.437, pred[10,128,5]{2,1,0:T(8,128)(4,1)S(1)} %copy.15, pred[10,128,5]{2,1,0:T(8,128)(4,1)S(1)} %copy.11), kind=kLoop, calls=%fused_computation.15 | loop fusion | flops 2457600 | bytes 9843200 | tf_op jit(solution)/shard_map/add | solution.py:94
  276.6 3.6 collective-permute-start.1
  320.6 3.6 collective-permute-start.23
  324.2 3.7 collective-permute-start.31
  327.9 8.3 %collective-permute-start.32 = (f32[80,512]{1,0:T(8,128)S(1)}, f32[80,512]{1,0:T(8,128)S(1)}, u32[]{:S(2)}, u32[]{:S(2)}) collective-permute-start(f32[80,512]{1,0:T(8,128)S(1)} %collective-permute-done.30), channel_id=1, source_target_pairs={{0,32},{16,48},{32,64},{48,80},{64,96},{80,112},{96,0},{112,16},{1... | collective-permute-start | bytes 491528 | tf_op jit(solution)/shard_map/ppermute | solution.py:123
  336.3 5.7 %collective-permute-start.34 = (f32[80,512]{1,0:T(8,128)S(1)}, f32[80,512]{1,0:T(8,128)S(1)}, u32[]{:S(2)}, u32[]{:S(2)}) collective-permute-start(f32[80,512]{1,0:T(8,128)S(1)} %collective-permute-done.30), channel_id=1, source_target_pairs={{0,64},{16,80},{32,96},{48,112},{64,0},{80,16},{96,32},{112,48},{1... | collective-permute-start | bytes 491528 | tf_op jit(solution)/shard_map/ppermute | solution.py:123
  343.1 4.0 collective-permute-done.33
  348.5 4.0 collective-permute-done.16
  353.5 4.8 %collective-permute-start.25 = (f32[80,512]{1,0:T(8,128)S(1)}, f32[80,512]{1,0:T(8,128)S(1)}, u32[]{:S(2)}, u32[]{:S(2)}) collective-permute-start(f32[80,512]{1,0:T(8,128)S(1)} %collective-permute-done.24), channel_id=1, source_target_pairs={{1,0},{2,1},{3,2},{4,3},{5,4},{6,5},{7,6},{8,7},{9,8},{10,9},{11,1... | collective-permute-start | bytes 491528 | tf_op jit(solution)/shard_map/ppermute | solution.py:27
  362.0 8.6 %collective-permute-done.18 = f32[80,512]{1,0:T(8,128)S(1)} collective-permute-done((f32[80,512]{1,0:T(8,128)S(1)}, f32[80,512]{1,0:T(8,128)S(1)}, u32[]{:S(2)}, u32[]{:S(2)}) %collective-permute-start.18) | collective-permute-done | bytes 163872 | tf_op jit(solution)/shard_map/ppermute | solution.py:25
  370.6 5.4 %collective-permute-start.26 = (f32[80,512]{1,0:T(8,128)S(1)}, f32[80,512]{1,0:T(8,128)}, u32[]{:S(2)}, u32[]{:S(2)}) collective-permute-start(f32[80,512]{1,0:T(8,128)S(1)} %collective-permute-done.25), channel_id=1, source_target_pairs={{1,0},{2,1},{3,2},{4,3},{5,4},{6,5},{7,6},{8,7},{9,8},{10,9},{11,1... | collective-permute-start | bytes 491528 | tf_op jit(solution)/shard_map/ppermute | solution.py:27
  379.3 5.5 %collective-permute-start.27 = (f32[80,512]{1,0:T(8,128)}, f32[80,512]{1,0:T(8,128)}, u32[]{:S(2)}, u32[]{:S(2)}) collective-permute-start(f32[80,512]{1,0:T(8,128)} %collective-permute-done.26), channel_id=1, source_target_pairs={{1,0},{2,1},{3,2},{4,3},{5,4},{6,5},{7,6},{8,7},{9,8},{10,9},{11,1... | collective-permute-start | bytes 491528 | tf_op jit(solution)/shard_map/ppermute | solution.py:27
  389.7 5.4 %collective-permute-start.28 = (f32[80,512]{1,0:T(8,128)}, f32[80,512]{1,0:T(8,128)S(1)}, u32[]{:S(2)}, u32[]{:S(2)}) collective-permute-start(f32[80,512]{1,0:T(8,128)} %collective-permute-done.27), channel_id=1, source_target_pairs={{1,0},{2,1},{3,2},{4,3},{5,4},{6,5},{7,6},{8,7},{9,8},{10,9},{11,1... | collective-permute-start | bytes 491528 | tf_op jit(solution)/shard_map/ppermute | solution.py:27
  398.5 5.6 %collective-permute-start.29 = (f32[80,512]{1,0:T(8,128)S(1)}, f32[80,512]{1,0:T(8,128)S(1)}, u32[]{:S(2)}, u32[]{:S(2)}) collective-permute-start(f32[80,512]{1,0:T(8,128)S(1)} %collective-permute-done.28), channel_id=1, source_target_pairs={{1,0},{2,1},{3,2},{4,3},{5,4},{6,5},{7,6},{8,7},{9,8},{10,9},{11,1... | collective-permute-start | bytes 491528 | tf_op jit(solution)/shard_map/ppermute | solution.py:27
  420.2 3.9 gather_fusion.3
  424.2 9.6 %convolution_subtract_fusion = f32[1280,640]{1,0:T(8,128)} fusion(f32[1280,640]{1,0:T(8,128)} %copy-done.1, f32[1280,512]{1,0:T(8,128)} %bitcast.107, f32[640,512]{1,0:T(8,128)S(1)} %bitcast.109), kind=kOutput, calls=%fused_computation.16 | convolution fusion | flops 5033984000 | bytes 10485760 | tf_op jit(solution)/shard_map/dot_general | solution.py:126
  (162 shorter events, 95.7 us)
Async XLA Ops:
  22.8 109.8 %all-to-all-start = ((f32[128,1,128,128]{3,2,1,0:T(8,128)}), f32[128,1,128,128]{3,2,1,0:T(8,128)}, u32[]{:S(2)}, u32[]{:S(2)}) async-start(f32[128,1,128,128]{3,2,1,0:T(8,128)} %fusion), calls=%async_computation | async-start | bytes 16777216 | tf_op jit(solution)/shard_map/all_to_all | solution.py:71
  273.9 12.1 %collective-permute-start = (f32[80,512]{1,0:T(8,128)S(1)}, f32[80,512]{1,0:T(8,128)S(1)}, u32[]{:S(2)}, u32[]{:S(2)}) collective-permute-start(f32[80,512]{1,0:T(8,128)S(1)} %get-tuple-element.19), channel_id=1, source_target_pairs={{0,1},{16,17},{32,33},{48,49},{64,65},{80,81},{96,97},{112,113}} | collective-permute-start | bytes 491528 | tf_op jit(solution)/shard_map/ppermute | solution.py:106
  276.6 10.8 %collective-permute-start.1 = (f32[80,512]{1,0:T(8,128)S(1)}, f32[80,512]{1,0:T(8,128)S(1)}, u32[]{:S(2)}, u32[]{:S(2)}) collective-permute-start(f32[80,512]{1,0:T(8,128)S(1)} %get-tuple-element.33), channel_id=1, source_target_pairs={{0,2},{16,18},{32,34},{48,50},{64,66},{80,82},{96,98},{112,114}} | collective-permute-start | bytes 491528 | tf_op jit(solution)/shard_map/ppermute | solution.py:106
  286.0 10.3 %collective-permute-start.13 = (f32[80,512]{1,0:T(8,128)S(1)}, f32[80,512]{1,0:T(8,128)S(1)}, u32[]{:S(2)}, u32[]{:S(2)}) collective-permute-start(f32[80,512]{1,0:T(8,128)S(1)} %get-tuple-element.21), channel_id=1, source_target_pairs={{0,14},{16,30},{32,46},{48,62},{64,78},{80,94},{96,110},{112,126}} | collective-permute-start | bytes 491528 | tf_op jit(solution)/shard_map/ppermute | solution.py:106
  287.3 11.2 %collective-permute-start.14 = (f32[80,512]{1,0:T(8,128)S(1)}, f32[80,512]{1,0:T(8,128)S(1)}, u32[]{:S(2)}, u32[]{:S(2)}) collective-permute-start(f32[80,512]{1,0:T(8,128)S(1)} %get-tuple-element.20), channel_id=1, source_target_pairs={{0,15},{16,31},{32,47},{48,63},{64,79},{80,95},{96,111},{112,127}} | collective-permute-start | bytes 491528 | tf_op jit(solution)/shard_map/ppermute | solution.py:106
  288.7 11.8 %collective-permute-start.2 = (f32[80,512]{1,0:T(8,128)S(1)}, f32[80,512]{1,0:T(8,128)S(1)}, u32[]{:S(2)}, u32[]{:S(2)}) collective-permute-start(f32[80,512]{1,0:T(8,128)S(1)} %get-tuple-element.32), channel_id=1, source_target_pairs={{0,3},{16,19},{32,35},{48,51},{64,67},{80,83},{96,99},{112,115}} | collective-permute-start | bytes 491528 | tf_op jit(solution)/shard_map/ppermute | solution.py:106
  290.0 12.5 %collective-permute-start.3 = (f32[80,512]{1,0:T(8,128)S(1)}, f32[80,512]{1,0:T(8,128)S(1)}, u32[]{:S(2)}, u32[]{:S(2)}) collective-permute-start(f32[80,512]{1,0:T(8,128)S(1)} %get-tuple-element.31), channel_id=1, source_target_pairs={{0,4},{16,20},{32,36},{48,52},{64,68},{80,84},{96,100},{112,116}} | collective-permute-start | bytes 491528 | tf_op jit(solution)/shard_map/ppermute | solution.py:106
  292.8 11.8 %collective-permute-start.4 = (f32[80,512]{1,0:T(8,128)S(1)}, f32[80,512]{1,0:T(8,128)S(1)}, u32[]{:S(2)}, u32[]{:S(2)}) collective-permute-start(f32[80,512]{1,0:T(8,128)S(1)} %get-tuple-element.30), channel_id=1, source_target_pairs={{0,5},{16,21},{32,37},{48,53},{64,69},{80,85},{96,101},{112,117}} | collective-permute-start | bytes 491528 | tf_op jit(solution)/shard_map/ppermute | solution.py:106
  296.3 10.3 %collective-permute-start.5 = (f32[80,512]{1,0:T(8,128)S(1)}, f32[80,512]{1,0:T(8,128)}, u32[]{:S(2)}, u32[]{:S(2)}) collective-permute-start(f32[80,512]{1,0:T(8,128)S(1)} %get-tuple-element.29), channel_id=1, source_target_pairs={{0,6},{16,22},{32,38},{48,54},{64,70},{80,86},{96,102},{112,118}} | collective-permute-start | bytes 491528 | tf_op jit(solution)/shard_map/ppermute | solution.py:106
  302.4 11.0 %collective-permute-start.8 = (f32[80,512]{1,0:T(8,128)S(1)}, f32[80,512]{1,0:T(8,128)}, u32[]{:S(2)}, u32[]{:S(2)}) collective-permute-start(f32[80,512]{1,0:T(8,128)S(1)} %get-tuple-element.26), channel_id=1, source_target_pairs={{0,9},{16,25},{32,41},{48,57},{64,73},{80,89},{96,105},{112,121}} | collective-permute-start | bytes 491528 | tf_op jit(solution)/shard_map/ppermute | solution.py:106
  304.6 11.1 %collective-permute-start.9 = (f32[80,512]{1,0:T(8,128)S(1)}, f32[80,512]{1,0:T(8,128)}, u32[]{:S(2)}, u32[]{:S(2)}) collective-permute-start(f32[80,512]{1,0:T(8,128)S(1)} %get-tuple-element.25), channel_id=1, source_target_pairs={{0,10},{16,26},{32,42},{48,58},{64,74},{80,90},{96,106},{112,122}} | collective-permute-start | bytes 491528 | tf_op jit(solution)/shard_map/ppermute | solution.py:106
  318.8 23.2 %collective-permute-start.15 = (f32[80,512]{1,0:T(8,128)S(1)}, f32[80,512]{1,0:T(8,128)S(1)}, u32[]{:S(2)}, u32[]{:S(2)}) collective-permute-start(f32[80,512]{1,0:T(8,128)S(1)} %fusion.16), channel_id=1, source_target_pairs={{0,1},{1,2},{2,3},{3,4},{4,5},{5,6},{6,7},{7,8},{8,9},{9,10},{10,1... | collective-permute-start | bytes 491528 | tf_op jit(solution)/shard_map/ppermute | solution.py:25
  320.6 21.6 %collective-permute-start.23 = (f32[80,512]{1,0:T(8,128)S(1)}, f32[80,512]{1,0:T(8,128)S(1)}, u32[]{:S(2)}, u32[]{:S(2)}) collective-permute-start(f32[80,512]{1,0:T(8,128)S(1)} %fusion.16), channel_id=1, source_target_pairs={{1,0},{2,1},{3,2},{4,3},{5,4},{6,5},{7,6},{8,7},{9,8},{10,9},{11,1... | collective-permute-start | bytes 491528 | tf_op jit(solution)/shard_map/ppermute | solution.py:27
  324.2 12.0 %collective-permute-start.31 = (f32[80,512]{1,0:T(8,128)S(1)}, f32[80,512]{1,0:T(8,128)S(1)}, u32[]{:S(2)}, u32[]{:S(2)}) collective-permute-start(f32[80,512]{1,0:T(8,128)S(1)} %collective-permute-done.30), channel_id=1, source_target_pairs={{0,16},{16,32},{32,48},{48,64},{64,80},{80,96},{96,112},{112,0},{1... | collective-permute-start | bytes 491528 | tf_op jit(solution)/shard_map/ppermute | solution.py:123
  327.9 14.2 %collective-permute-start.32 = (f32[80,512]{1,0:T(8,128)S(1)}, f32[80,512]{1,0:T(8,128)S(1)}, u32[]{:S(2)}, u32[]{:S(2)}) collective-permute-start(f32[80,512]{1,0:T(8,128)S(1)} %collective-permute-done.30), channel_id=1, source_target_pairs={{0,32},{16,48},{32,64},{48,80},{64,96},{80,112},{96,0},{112,16},{1... | collective-permute-start | bytes 491528 | tf_op jit(solution)/shard_map/ppermute | solution.py:123
  336.2 10.9 %collective-permute-start.33 = (f32[80,512]{1,0:T(8,128)S(1)}, f32[80,512]{1,0:T(8,128)S(1)}, u32[]{:S(2)}, u32[]{:S(2)}) collective-permute-start(f32[80,512]{1,0:T(8,128)S(1)} %collective-permute-done.30), channel_id=1, source_target_pairs={{0,48},{16,64},{32,80},{48,96},{64,112},{80,0},{96,16},{112,32},{1... | collective-permute-start | bytes 491528 | tf_op jit(solution)/shard_map/ppermute | solution.py:123
  336.3 16.2 %collective-permute-start.34 = (f32[80,512]{1,0:T(8,128)S(1)}, f32[80,512]{1,0:T(8,128)S(1)}, u32[]{:S(2)}, u32[]{:S(2)}) collective-permute-start(f32[80,512]{1,0:T(8,128)S(1)} %collective-permute-done.30), channel_id=1, source_target_pairs={{0,64},{16,80},{32,96},{48,112},{64,0},{80,16},{96,32},{112,48},{1... | collective-permute-start | bytes 491528 | tf_op jit(solution)/shard_map/ppermute | solution.py:123
  342.0 28.6 %collective-permute-start.35 = (f32[80,512]{1,0:T(8,128)S(1)}, f32[80,512]{1,0:T(8,128)S(1)}, u32[]{:S(2)}, u32[]{:S(2)}) collective-permute-start(f32[80,512]{1,0:T(8,128)S(1)} %collective-permute-done.30), channel_id=1, source_target_pairs={{0,80},{16,96},{32,112},{48,0},{64,16},{80,32},{96,48},{112,64},{1... | collective-permute-start | bytes 491528 | tf_op jit(solution)/shard_map/ppermute | solution.py:123
  342.1 10.4 %collective-permute-start.16 = (f32[80,512]{1,0:T(8,128)S(1)}, f32[80,512]{1,0:T(8,128)S(1)}, u32[]{:S(2)}, u32[]{:S(2)}) collective-permute-start(f32[80,512]{1,0:T(8,128)S(1)} %collective-permute-done.15), channel_id=1, source_target_pairs={{0,1},{1,2},{2,3},{3,4},{4,5},{5,6},{6,7},{7,8},{8,9},{9,10},{10,1... | collective-permute-start | bytes 491528 | tf_op jit(solution)/shard_map/ppermute | solution.py:25
  342.2 37.0 %collective-permute-start.36 = (f32[80,512]{1,0:T(8,128)S(1)}, f32[80,512]{1,0:T(8,128)S(1)}, u32[]{:S(2)}, u32[]{:S(2)}) collective-permute-start(f32[80,512]{1,0:T(8,128)S(1)} %collective-permute-done.30), channel_id=1, source_target_pairs={{0,96},{16,112},{32,0},{48,16},{64,32},{80,48},{96,64},{112,80},{1... | collective-permute-start | bytes 491528 | tf_op jit(solution)/shard_map/ppermute | solution.py:123
  352.5 35.5 %collective-permute-start.37 = (f32[80,512]{1,0:T(8,128)S(1)}, f32[80,512]{1,0:T(8,128)S(1)}, u32[]{:S(2)}, u32[]{:S(2)}) collective-permute-start(f32[80,512]{1,0:T(8,128)S(1)} %collective-permute-done.30), channel_id=1, source_target_pairs={{0,112},{16,0},{32,16},{48,32},{64,48},{80,64},{96,80},{112,96},{1... | collective-permute-start | bytes 491528 | tf_op jit(solution)/shard_map/ppermute | solution.py:123
  353.5 17.1 %collective-permute-start.25 = (f32[80,512]{1,0:T(8,128)S(1)}, f32[80,512]{1,0:T(8,128)S(1)}, u32[]{:S(2)}, u32[]{:S(2)}) collective-permute-start(f32[80,512]{1,0:T(8,128)S(1)} %collective-permute-done.24), channel_id=1, source_target_pairs={{1,0},{2,1},{3,2},{4,3},{5,4},{6,5},{7,6},{8,7},{9,8},{10,9},{11,1... | collective-permute-start | bytes 491528 | tf_op jit(solution)/shard_map/ppermute | solution.py:27
  379.3 10.4 %collective-permute-start.27 = (f32[80,512]{1,0:T(8,128)}, f32[80,512]{1,0:T(8,128)}, u32[]{:S(2)}, u32[]{:S(2)}) collective-permute-start(f32[80,512]{1,0:T(8,128)} %collective-permute-done.26), channel_id=1, source_target_pairs={{1,0},{2,1},{3,2},{4,3},{5,4},{6,5},{7,6},{8,7},{9,8},{10,9},{11,1... | collective-permute-start | bytes 491528 | tf_op jit(solution)/shard_map/ppermute | solution.py:27
  398.5 21.1 %collective-permute-start.29 = (f32[80,512]{1,0:T(8,128)S(1)}, f32[80,512]{1,0:T(8,128)S(1)}, u32[]{:S(2)}, u32[]{:S(2)}) collective-permute-start(f32[80,512]{1,0:T(8,128)S(1)} %collective-permute-done.28), channel_id=1, source_target_pairs={{1,0},{2,1},{3,2},{4,3},{5,4},{6,5},{7,6},{8,7},{9,8},{10,9},{11,1... | collective-permute-start | bytes 491528 | tf_op jit(solution)/shard_map/ppermute | solution.py:27
  (23 other events, 524.4 us)
